TPU v7x, 32 devices: a whole 2x2x4 slice. The times are simulated.
32 devices in a mesh: row: 8 (over z, core), col: 4 (over y, x).
Axes of the slice: x: 2, y: 2, z: 4, core: 2. Of those that a mesh axis runs over, the one named last changes fastest.
Arguments:
- activations: bfloat16 [1024, 8192], P('col', 'row'), may hold values from -6 to 6
- out_grad: bfloat16 [1024, 8192], P('col', 'row'), may hold values from -6 to 6
- gate_pre: bfloat16 [1024, 16384], P('row', 'col'), may hold values from -8 to 8
- up_proj: bfloat16 [1024, 16384], P('row', 'col'), may hold values from -6 to 6
- gate_weight: bfloat16 [8192, 16384], P('row', 'col'), may hold values from -0.0625 to 0.0625
- up_weight: bfloat16 [8192, 16384], P('row', 'col'), may hold values from -0.0625 to 0.0625
- down_weight: bfloat16 [16384, 8192], P('col', 'row'), may hold values from -0.046875 to 0.046875
Outputs:
- input_grad: bfloat16 [1024, 8192], P('col', 'row')
- gate_grad: bfloat16 [8192, 16384], P('row', 'col')
- up_grad: bfloat16 [8192, 16384], P('row', 'col')
- down_grad: bfloat16 [16384, 8192], P('col', 'row')
All inputs are finite; a program needn't handle non-finite values.
Results may differ from a plain program's by a relative error of at most 0.0051.
Values may be sent and summed in bfloat16 or wider, within the bound.
No kernel may reach another device: no remote copies, remote signals or barrier semaphores. Data moves between devices by JAX's collectives and lax.ppermute only.
A program may use at most 192 MiB of HBM per device.

v0:
```python
import jax
import jax.numpy as jnp
from jax import lax
from jax.sharding import PartitionSpec as P


def local_grads(gate_rows, up_rows, grad_rows):
    gate_float = gate_rows.astype(jnp.float32)
    up_float = up_rows.astype(jnp.float32)
    sigmoid_gate = jax.nn.sigmoid(gate_float)
    silu_gate = gate_float * sigmoid_gate
    hidden_act = (silu_gate * up_float).astype(jnp.bfloat16)
    gate_delta = (
        grad_rows * up_float * sigmoid_gate * (1.0 + gate_float * (1.0 - sigmoid_gate))
    ).astype(jnp.bfloat16)
    up_delta = (grad_rows * silu_gate).astype(jnp.bfloat16)
    return (hidden_act, gate_delta, up_delta)


def body(activations, out_grad, gate_pre, up_proj, gate_weight, up_weight, down_weight):
    act_full, grad_full = (
        lax.all_gather(activations, "col", axis=0, tiled=True),
        lax.all_gather(out_grad, "col", axis=0, tiled=True),
    )
    tokens_all = act_full.shape[0]
    contract_last = (((1,), (1,)), ((), ()))
    contract_first = (((0,), (0,)), ((), ()))
    grad_rows = grad_full
    hid_rows = lax.psum_scatter(
        lax.dot_general(grad_rows, down_weight, contract_last, preferred_element_type=jnp.float32),
        "row",
        scatter_dimension=0,
        tiled=True,
    )
    products = local_grads(gate_pre, up_proj, hid_rows)
    hidden_act = lax.all_gather(products[0], "row", axis=0, tiled=True)
    gate_delta = lax.all_gather(products[1], "row", axis=0, tiled=True)
    up_delta = lax.all_gather(products[2], "row", axis=0, tiled=True)
    grad_rows = grad_full
    acc_down = lax.dot_general(
        hidden_act, grad_rows, contract_first, preferred_element_type=jnp.float32
    )
    acc_gate = lax.dot_general(
        act_full, gate_delta, contract_first, preferred_element_type=jnp.float32
    )
    acc_up = lax.dot_general(act_full, up_delta, contract_first, preferred_element_type=jnp.float32)
    input_rows = lax.dot_general(
        gate_delta, gate_weight, contract_last, preferred_element_type=jnp.float32
    )
    input_rows = input_rows + lax.dot_general(
        up_delta, up_weight, contract_last, preferred_element_type=jnp.float32
    )
    acc_input = input_rows
    totals = (acc_down, acc_gate, acc_up, acc_input)
    acc_down, acc_gate, acc_up, acc_input = totals
    input_rows = lax.psum_scatter(acc_input, "col", scatter_dimension=0, tiled=True).astype(
        jnp.bfloat16
    )
    factor = float(tokens_all) ** (-0.5)
    return (
        input_rows,
        (acc_gate * factor).astype(jnp.bfloat16),
        (acc_up * factor).astype(jnp.bfloat16),
        (acc_down * factor).astype(jnp.bfloat16),
    )


def solution(mesh):
    in_specs = (
        P("col", "row"),
        P("col", "row"),
        P("row", "col"),
        P("row", "col"),
        P("row", "col"),
        P("row", "col"),
        P("col", "row"),
    )
    out_specs = (P("col", "row"), P("row", "col"), P("row", "col"), P("col", "row"))
    return jax.shard_map(body, mesh=mesh, in_specs=in_specs, out_specs=out_specs, check_vma=False)
```

profile of v0, /device:TPU:0, one launch (start us, length us, event | category | flops | bytes accessed | tf_op | source)
XLA Modules:
  0.0 582.2 jit_solution(11149804209979248327)
XLA Ops:
  7.2 0.0 all-gather.6.cloned.1.call-start
  7.2 0.7 all-gather.6.cloned.1.call-update
  7.9 0.0 reduce-scatter.3.cloned.1.call-start
  7.9 39.9 %all-gather.6.cloned.1.call-done = bf16[1024,1024]{1,0:T(8,128)(2,1)} async-done(((bf16[256,1024]{1,0:T(8,128)(2,1)}), bf16[1024,1024]{1,0:T(8,128)(2,1)}) %all-gather.6.cloned.1.call-update) | async-done | bytes 2097168 | tf_op jit(solution)/shard_map/all_gather | solution.py:23
  47.9 16.0 %fusion.10 = f32[1024,4096]{1,0:T(8,128)} fusion(bf16[1024,1024]{1,0:T(8,128)(2,1)} %all-gather.6.cloned.1.call-done, bf16[4096,1024]{1,0:T(8,128)(2,1)} %param.13), kind=kOutput, calls=%fused_computation.20 | convolution fusion | flops 8589934592 | bytes 27262976 | tf_op jit(solution)/shard_map/dot_general | solution.py:30
  63.9 0.0 reduce-scatter.3.cloned.1.call-update
  64.0 0.0 all-gather.8.cloned.1.call-start
  64.0 168.3 %reduce-scatter.3.cloned.1.call-done = f32[128,4096]{1,0:T(8,128)} async-done(((f32[1024,4096]{1,0:T(8,128)}), f32[128,4096]{1,0:T(8,128)}) %reduce-scatter.3.cloned.1.call-update) | async-done | bytes 2097168 | tf_op jit(solution)/shard_map/reduce_scatter | solution.py:29
  232.4 0.0 copy-done
  232.4 4.4 multiply_convert_fusion.3
  236.7 0.0 all-gather.8.cloned.1.call-update
  236.8 0.0 all-gather.10.cloned.1.call-start
  236.8 0.5 all-gather.10.cloned.1.call-update
  237.3 0.0 all-gather.12.cloned.1.call-start
  237.4 0.5 all-gather.12.cloned.1.call-update
  237.9 0.0 all-gather.14.cloned.1.call-start
  238.0 0.5 all-gather.14.cloned.1.call-update
  238.5 0.2 reduce-scatter.5.cloned.1.call-start
  238.7 78.6 %all-gather.8.cloned.1.call-done = bf16[1024,4096]{1,0:T(8,128)(2,1)} async-done(((bf16[128,4096]{1,0:T(8,128)(2,1)}), bf16[1024,4096]{1,0:T(8,128)(2,1)}) %all-gather.8.cloned.1.call-update) | async-done | bytes 8388624 | tf_op jit(solution)/shard_map/all_gather | solution.py:37
  317.3 15.0 %fusion.11 = f32[1024,1024]{1,0:T(8,128)} fusion(bf16[1024,4096]{1,0:T(8,128)(2,1)} %all-gather.8.cloned.1.call-done, bf16[1024,4096]{1,0:T(8,128)(2,1)} %param.11), kind=kOutput, calls=%fused_computation.21 | convolution fusion | flops 8589934592 | bytes 20971520 | tf_op jit(solution)/shard_map/dot_general | solution.py:47
  332.3 67.6 %all-gather.10.cloned.1.call-done = bf16[1024,4096]{1,0:T(8,128)(2,1)} async-done(((bf16[128,4096]{1,0:T(8,128)(2,1)}), bf16[1024,4096]{1,0:T(8,128)(2,1)}) %all-gather.10.cloned.1.call-update) | async-done | bytes 8388624 | tf_op jit(solution)/shard_map/all_gather | solution.py:38
  400.0 15.7 %convolution_add_fusion = f32[1024,1024]{1,0:T(8,128)} fusion(f32[1024,1024]{1,0:T(8,128)} %fusion.11, bf16[1024,4096]{1,0:T(8,128)(2,1)} %all-gather.10.cloned.1.call-done, bf16[1024,4096]{1,0:T(8,128)(2,1)} %param.12), kind=kOutput, calls=%fused_computation.19 | convolution fusion | flops 8590983168 | bytes 25165824 | tf_op jit(solution)/shard_map/dot_general | solution.py:50
  415.7 0.0 reduce-scatter.5.cloned.1.call-update
  415.7 19.8 %all-gather.12.cloned.1.call-done = bf16[1024,1024]{1,0:T(8,128)(2,1)} async-done(((bf16[256,1024]{1,0:T(8,128)(2,1)}), bf16[1024,1024]{1,0:T(8,128)(2,1)}) %all-gather.12.cloned.1.call-update) | async-done | bytes 2097168 | tf_op jit(solution)/shard_map/all_gather | solution.py:22
  435.5 14.9 %fusion = bf16[1024,4096]{0,1:T(8,128)(2,1)} fusion(bf16[1024,4096]{1,0:T(8,128)(2,1)} %all-gather.8.cloned.1.call-done, bf16[1024,1024]{1,0:T(8,128)(2,1)} %all-gather.12.cloned.1.call-done), kind=kOutput, calls=%fused_computation.3 | convolution fusion | flops 8598323200 | bytes 18874368 | tf_op jit(solution)/shard_map/dot_general | solution.py:43
  450.4 12.1 %copy.11 = bf16[1024,4096]{1,0:T(8,128)(2,1)} copy(bf16[1024,4096]{0,1:T(8,128)(2,1)} %fusion) | data formatting | bytes 16777216
  462.5 14.7 %fusion.1 = bf16[1024,4096]{0,1:T(8,128)(2,1)} fusion(bf16[1024,4096]{1,0:T(8,128)(2,1)} %all-gather.10.cloned.1.call-done, bf16[1024,1024]{1,0:T(8,128)(2,1)S(1)} %copy-done.3), kind=kOutput, calls=%fused_computation.4 | convolution fusion | flops 8598323200 | bytes 18874368 | tf_op jit(solution)/shard_map/dot_general | solution.py:46
  477.2 12.1 %copy.12 = bf16[1024,4096]{1,0:T(8,128)(2,1)} copy(bf16[1024,4096]{0,1:T(8,128)(2,1)} %fusion.1) | data formatting | bytes 16777216
  489.3 29.8 %all-gather.14.cloned.1.call-done = bf16[1024,4096]{1,0:T(8,128)(2,1)} async-done(((bf16[128,4096]{1,0:T(8,128)(2,1)}), bf16[1024,4096]{1,0:T(8,128)(2,1)}) %all-gather.14.cloned.1.call-update) | async-done | bytes 8388624 | tf_op jit(solution)/shard_map/all_gather | solution.py:36
  519.1 14.6 %multiply_convert_fusion = bf16[4096,1024]{1,0:T(8,128)(2,1)} fusion(bf16[1024,4096]{1,0:T(8,128)(2,1)} %all-gather.14.cloned.1.call-done, bf16[1024,1024]{1,0:T(8,128)(2,1)S(1)} %copy-done.2), kind=kOutput, calls=%fused_computation | convolution fusion | flops 8598323200 | bytes 18874368 | tf_op jit(solution)/shard_map/dot_general | solution.py:40
  533.6 39.7 %reduce-scatter.5.cloned.1.call-done = f32[256,1024]{1,0:T(8,128)} async-done(((f32[1024,1024]{1,0:T(8,128)}), f32[256,1024]{1,0:T(8,128)}) %reduce-scatter.5.cloned.1.call-update) | async-done | bytes 1048592 | tf_op jit(solution)/shard_map/reduce_scatter | solution.py:56
  573.3 2.1 convert_element_type.37
  (7 shorter events, 0.0 us)
Async XLA Ops:
  7.2 40.7 %all-gather.6.cloned.1.call-start = ((), (), s32[]{:S(2)}) async-start(), calls=%async_computation.2 | async-start | bytes 2621440 | tf_op jit(solution)/shard_map/all_gather | solution.py:23
  7.9 224.5 %reduce-scatter.3.cloned.1.call-start = ((), (), s32[]{:S(2)}) async-start(), calls=%async_computation.3 | async-start | bytes 18874368 | tf_op jit(solution)/shard_map/reduce_scatter | solution.py:29
  63.9 168.4 %copy-start = (bf16[128,4096]{1,0:T(8,128)(2,1)S(1)}, bf16[128,4096]{1,0:T(8,128)(2,1)}, u32[]{:S(2)}) copy-start(bf16[128,4096]{1,0:T(8,128)(2,1)} %param.9) | copy-start | bytes 3145732
  63.9 168.4 %copy-start.1 = (bf16[128,4096]{1,0:T(8,128)(2,1)S(1)}, bf16[128,4096]{1,0:T(8,128)(2,1)}, u32[]{:S(2)}) copy-start(bf16[128,4096]{1,0:T(8,128)(2,1)} %param.10) | copy-start | bytes 3145732
  64.0 253.3 %all-gather.8.cloned.1.call-start = ((), (), s32[]{:S(2)}) async-start(), calls=%async_computation.4 | async-start | bytes 9437184 | tf_op jit(solution)/shard_map/all_gather | solution.py:37
  236.8 163.2 %all-gather.10.cloned.1.call-start = ((), (), s32[]{:S(2)}) async-start(), calls=%async_computation.5 | async-start | bytes 9437184 | tf_op jit(solution)/shard_map/all_gather | solution.py:38
  237.3 198.2 %all-gather.12.cloned.1.call-start = ((), (), s32[]{:S(2)}) async-start(), calls=%async_computation.7 | async-start | bytes 2621440 | tf_op jit(solution)/shard_map/all_gather | solution.py:22
  237.9 281.1 %all-gather.14.cloned.1.call-start = ((), (), s32[]{:S(2)}) async-start(), calls=%async_computation.8 | async-start | bytes 9437184 | tf_op jit(solution)/shard_map/all_gather | solution.py:36
  238.5 334.8 %reduce-scatter.5.cloned.1.call-start = ((), (), s32[]{:S(2)}) async-start(), calls=%async_computation.6 | async-start | bytes 5242880 | tf_op jit(solution)/shard_map/reduce_scatter | solution.py:56
  450.4 12.1 %copy-start.3 = (bf16[1024,1024]{1,0:T(8,128)(2,1)S(1)}, bf16[1024,1024]{1,0:T(8,128)(2,1)}, u32[]{:S(2)}) copy-start(bf16[1024,1024]{1,0:T(8,128)(2,1)} %all-gather.12.cloned.1.call-done) | copy-start | bytes 6291460
  477.2 41.9 %copy-start.2 = (bf16[1024,1024]{1,0:T(8,128)(2,1)S(1)}, bf16[1024,1024]{1,0:T(8,128)(2,1)}, u32[]{:S(2)}) copy-start(bf16[1024,1024]{1,0:T(8,128)(2,1)} %all-gather.6.cloned.1.call-done) | copy-start | bytes 6291460
Sparse Core Ops, SparseCore 0:
  9.8 38.0 all-gather.5
  64.1 168.2 reduce-scatter.2
  236.9 80.3 all-gather.7
  319.3 80.5 all-gather.9
  401.6 33.8 all-gather.11
  437.0 82.0 all-gather.13
  522.0 51.2 reduce-scatter.4
where the time goes:
time: 583 us; the launch traced here: 582 us
  waiting for transfers between devices  446 us (77%)
  matrix products  90.9 us (16%)
  local copies, waits for them, and re-layouts  24.2 us (4%)
  between operations  14.1 us (2%)
  other arithmetic  6.46 us (1%)
    reduce_scatter x1, waiting for transfers between devices, body(): lax.psum_scatter(lax.dot_general(grad_rows, down_weight, contract_last, p...  168 us
    all_gather x1, waiting for transfers between devices, body(): gate_delta = lax.all_gather(products[1], 'row', axis=0, tiled=True)  78.6 us
    all_gather x1, waiting for transfers between devices, body(): up_delta = lax.all_gather(products[2], 'row', axis=0, tiled=True)  67.6 us
    all_gather x1, waiting for transfers between devices, body(): lax.all_gather(out_grad, 'col', axis=0, tiled=True)  39.9 us
    reduce_scatter x1, waiting for transfers between devices, body(): lax.psum_scatter(acc_input, 'col', scatter_dimension=0, tiled=True)  39.7 us
    all_gather x1, waiting for transfers between devices, body(): hidden_act = lax.all_gather(products[0], 'row', axis=0, tiled=True)  29.8 us
    unnamed x10, local copies, waits for them, and re-layouts  24.2 us
    all_gather x1, waiting for transfers between devices, body(): lax.all_gather(activations, 'col', axis=0, tiled=True)  19.8 us
  transfers between devices with their start and end apart: 7, of which 7 were waited for; matrix products, arithmetic and copies ran while one was open for 17% of the time, Pallas kernels for 0%

commit v1 on v0

--- a/solution.py
+++ b/solution.py
@@ -2,6 +2,28 @@
 import jax.numpy as jnp
 from jax import lax
 from jax.sharding import PartitionSpec as P
+
+
+def in_order(parts, dim):
+    lengths = list(parts.shape[1:])
+    lengths[dim] *= parts.shape[0]
+    return jnp.moveaxis(parts, 0, dim).reshape(lengths)
+
+
+def gather_around(x, axis, dim):
+    size = lax.axis_size(axis)
+    pairs = [(i, (i + 1) % size) for i in range(size)]
+    back = [(b, a) for a, b in pairs]
+    lower, upper = ([], [])
+    for step in range(size - 1):
+        if step % 2 == 0:
+            lower.append(lax.ppermute(lower[-1] if lower else x, axis, pairs))
+        else:
+            upper.append(lax.ppermute(upper[-1] if upper else x, axis, back))
+    blocks = jnp.stack([*lower[::-1], x, *upper])
+    shift = lax.axis_index(axis) - len(lower)
+    blocks = blocks[(jnp.arange(size) - shift) % size]
+    return in_order(blocks, dim)
 
 
 def local_grads(gate_rows, up_rows, grad_rows):
@@ -35,7 +57,7 @@
     products = local_grads(gate_pre, up_proj, hid_rows)
     hidden_act = lax.all_gather(products[0], "row", axis=0, tiled=True)
     gate_delta = lax.all_gather(products[1], "row", axis=0, tiled=True)
-    up_delta = lax.all_gather(products[2], "row", axis=0, tiled=True)
+    up_delta = gather_around(products[2], "row", 0)
     grad_rows = grad_full
     acc_down = lax.dot_general(
         hidden_act, grad_rows, contract_first, preferred_element_type=jnp.float32

time: 583 us -> 550 us (0.943)
  waiting for transfers between devices: 446 us -> 386 us
  local copies, waits for them, and re-layouts: 24.2 us -> 45.7 us
  starting transfers between devices: 0.45 us -> 11.1 us
    ppermute x0 -> x7, waiting for transfers between devices: none -> 129 us  [the longest x4 120 us: gather_around(): lower.append(lax.ppermute(lower[-1] if lower else x, axis, pairs))]
    all_gather x1, waiting for transfers between devices: 78.6 us -> 0.01 us  [body(): gate_delta = lax.all_gather(products[1], 'row', axis=0, tiled=True)]
    all_gather x1 -> x0, waiting for transfers between devices: 67.6 us -> none  [body(): up_delta = lax.all_gather(products[2], 'row', axis=0, tiled=True)]
    all_gather x1, waiting for transfers between devices: 29.8 us -> 7.87 us  [body(): hidden_act = lax.all_gather(products[0], 'row', axis=0, tiled=True)]
    all_gather x1, waiting for transfers between devices: 19.8 us -> 0.02 us  [body(): lax.all_gather(activations, 'col', axis=0, tiled=True)]
    unnamed x10 -> x19, local copies, waits for them, and re-layouts: 24.2 us -> 36.4 us
    ppermute x0 -> x7, starting transfers between devices: none -> 10.9 us  [the longest x3 10.8 us: gather_around(): upper.append(lax.ppermute(upper[-1] if upper else x, axis, back))]
    gather x0 -> x1, local copies, waits for them, and re-layouts: none -> 8.23 us  [gather_around(): blocks = blocks[(jnp.arange(size) - shift) % size]]
  transfers between devices with their start and end apart: 7 -> 13, of which waited for: 7 -> 9; matrix products, arithmetic and copies ran while one was open for 17% -> 21% of each run, Pallas kernels for 0% -> 0%
where the time goes in v1:
time: 550 us
  waiting for transfers between devices  386 us (70%)
  matrix products  86.3 us (16%)
  local copies, waits for them, and re-layouts  45.7 us (8%)
  between operations  14.2 us (3%)
  starting transfers between devices  11.1 us (2%)
  other arithmetic  6.26 us (1%)
    reduce_scatter x1, waiting for transfers between devices, body(): lax.psum_scatter(lax.dot_general(grad_rows, down_weight, contract_last, p...  168 us
    ppermute x4, waiting for transfers between devices, gather_around(): lower.append(lax.ppermute(lower[-1] if lower else x, axis, pairs))  120 us
    all_gather x1, waiting for transfers between devices, body(): lax.all_gather(out_grad, 'col', axis=0, tiled=True)  39.9 us
    reduce_scatter x1, waiting for transfers between devices, body(): lax.psum_scatter(acc_input, 'col', scatter_dimension=0, tiled=True)  39.5 us
    unnamed x19, local copies, waits for them, and re-layouts  36.4 us
    dot_general x1, matrix products, body(): lax.dot_general(grad_rows, down_weight, contract_last, preferred_element_...  16 us
    dot_general x1, matrix products, body(): lax.dot_general(act_full, up_delta, contract_first, preferred_element_typ...  15.2 us
    dot_general x1, matrix products, body(): lax.dot_general(act_full, gate_delta, contract_first, preferred_element_t...  14.7 us
  transfers between devices with their start and end apart: 13, of which 9 were waited for; matrix products, arithmetic and copies ran while one was open for 21% of the time, Pallas kernels for 0%

profile of v1, /device:TPU:0, one launch (start us, length us, event | category | flops | bytes accessed | tf_op | source)
XLA Modules:
  0.0 549.5 jit_solution(125617500321907077)
XLA Ops:
  7.2 0.7 all-gather.5.cloned.1.call-update
  7.9 39.9 %all-gather.5.cloned.1.call-done = bf16[1024,1024]{1,0:T(8,128)(2,1)} async-done(((bf16[256,1024]{1,0:T(8,128)(2,1)}), bf16[1024,1024]{1,0:T(8,128)(2,1)}) %all-gather.5.cloned.1.call-update) | async-done | bytes 2097168 | tf_op jit(solution)/shard_map/all_gather | solution.py:45
  47.9 16.0 %fusion.12 = f32[1024,4096]{1,0:T(8,128)} fusion(bf16[1024,1024]{1,0:T(8,128)(2,1)} %all-gather.5.cloned.1.call-done, bf16[4096,1024]{1,0:T(8,128)(2,1)} %param.13), kind=kOutput, calls=%fused_computation.36 | convolution fusion | flops 8589934592 | bytes 27262976 | tf_op jit(solution)/shard_map/dot_general | solution.py:52
  64.0 168.3 %reduce-scatter.3.cloned.1.call-done = f32[128,4096]{1,0:T(8,128)} async-done(((f32[1024,4096]{1,0:T(8,128)}), f32[128,4096]{1,0:T(8,128)}) %reduce-scatter.3.cloned.1.call-update) | async-done | bytes 2097168 | tf_op jit(solution)/shard_map/reduce_scatter | solution.py:51
  232.4 4.1 multiply_convert_fusion.3
  237.2 26.8 %collective-permute-done = bf16[128,4096]{1,0:T(8,128)(2,1)S(1)} collective-permute-done((bf16[128,4096]{1,0:T(8,128)(2,1)S(1)}, bf16[128,4096]{1,0:T(8,128)(2,1)S(1)}, u32[]{:S(2)}, u32[]{:S(2)}) %collective-permute-start) | collective-permute-done | bytes 1048608 | tf_op jit(solution)/shard_map/ppermute | solution.py:20
  264.1 3.6 collective-permute-start.4
  267.6 45.6 %collective-permute-done.1 = bf16[128,4096]{1,0:T(8,128)(2,1)S(1)} collective-permute-done((bf16[128,4096]{1,0:T(8,128)(2,1)S(1)}, bf16[128,4096]{1,0:T(8,128)(2,1)S(1)}, u32[]{:S(2)}, u32[]{:S(2)}) %collective-permute-start.1) | collective-permute-done | bytes 1048608 | tf_op jit(solution)/shard_map/ppermute | solution.py:20
  313.3 3.5 collective-permute-start.5
  316.8 36.1 %collective-permute-done.2 = bf16[128,4096]{1,0:T(8,128)(2,1)} collective-permute-done((bf16[128,4096]{1,0:T(8,128)(2,1)S(1)}, bf16[128,4096]{1,0:T(8,128)(2,1)}, u32[]{:S(2)}, u32[]{:S(2)}) %collective-permute-start.2) | collective-permute-done | bytes 1048608 | tf_op jit(solution)/shard_map/ppermute | solution.py:20
  353.0 9.0 %collective-permute-done.5 = bf16[128,4096]{1,0:T(8,128)(2,1)} collective-permute-done((bf16[128,4096]{1,0:T(8,128)(2,1)}, bf16[128,4096]{1,0:T(8,128)(2,1)}, u32[]{:S(2)}, u32[]{:S(2)}) %collective-permute-start.5) | collective-permute-done | bytes 1048608 | tf_op jit(solution)/shard_map/ppermute | solution.py:22
  362.0 3.7 collective-permute-start.6
  365.7 11.4 %collective-permute-done.3 = bf16[128,4096]{1,0:T(8,128)(2,1)} collective-permute-done((bf16[128,4096]{1,0:T(8,128)(2,1)}, bf16[128,4096]{1,0:T(8,128)(2,1)}, u32[]{:S(2)}, u32[]{:S(2)}) %collective-permute-start.3) | collective-permute-done | bytes 1048608 | tf_op jit(solution)/shard_map/ppermute | solution.py:20
  377.1 2.3 bitcast_dynamic-update-slice_fusion.7
  379.4 2.3 bitcast_dynamic-update-slice_fusion.6
  381.7 1.0 bitcast_dynamic-update-slice_fusion.5
  382.7 1.0 bitcast_dynamic-update-slice_fusion.4
  383.8 1.0 bitcast_dynamic-update-slice_fusion.3
  384.8 2.3 bitcast_dynamic-update-slice_fusion.2
  387.1 2.3 bitcast_dynamic-update-slice_fusion.1
  389.4 1.0 bitcast_dynamic-update-slice_fusion
  390.4 8.2 %gather_fusion = bf16[8,128,4096]{2,1,0:T(8,128)(2,1)} fusion(bf16[8,128,4096]{2,1,0:T(8,128)(2,1)} %bitcast_dynamic-update-slice_fusion, s32[1024]{0:T(1024)S(1)} %pad_clamp_fusion), kind=kCustom, calls=%fused_computation | custom fusion | bytes 16777248 | tf_op jit(solution)/shard_map/gather | solution.py:25
  398.7 12.8 %fusion.13 = f32[1024,1024]{1,0:T(8,128)S(1)} fusion(bf16[1024,4096]{1,0:T(8,128)(2,1)} %all-gather.7.cloned.1.call-done, bf16[1024,4096]{1,0:T(8,128)(2,1)} %param.11), kind=kOutput, calls=%fused_computation.37 | convolution fusion | flops 8589934592 | bytes 20971520 | tf_op jit(solution)/shard_map/dot_general | solution.py:69
  411.5 13.0 %convolution_add_fusion = f32[1024,1024]{1,0:T(8,128)} fusion(f32[1024,1024]{1,0:T(8,128)S(1)} %fusion.13, bf16[1024,4096]{1,0:T(8,128)(2,1)S(1)} %bitcast.36, bf16[1024,4096]{1,0:T(8,128)(2,1)} %param.12), kind=kOutput, calls=%fused_computation.20 | convolution fusion | flops 8590983168 | bytes 25165824 | tf_op jit(solution)/shard_map/dot_general | solution.py:72
  424.6 15.2 %fusion.1 = bf16[1024,4096]{0,1:T(8,128)(2,1)} fusion(bf16[1024,4096]{1,0:T(8,128)(2,1)} %bitcast.35, bf16[1024,1024]{1,0:T(8,128)(2,1)} %all-gather.9.cloned.1.call-done), kind=kOutput, calls=%fused_computation.5 | convolution fusion | flops 8598323200 | bytes 18874368 | tf_op jit(solution)/shard_map/dot_general | solution.py:68
  439.8 12.1 %copy.12 = bf16[1024,4096]{1,0:T(8,128)(2,1)} copy(bf16[1024,4096]{0,1:T(8,128)(2,1)} %fusion.1) | data formatting | bytes 16777216
  451.9 14.7 %fusion = bf16[1024,4096]{0,1:T(8,128)(2,1)} fusion(bf16[1024,4096]{1,0:T(8,128)(2,1)} %all-gather.7.cloned.1.call-done, bf16[1024,1024]{1,0:T(8,128)(2,1)S(1)} %copy-done.4), kind=kOutput, calls=%fused_computation.4 | convolution fusion | flops 8598323200 | bytes 18874368 | tf_op jit(solution)/shard_map/dot_general | solution.py:65
  466.6 12.1 %copy.11 = bf16[1024,4096]{1,0:T(8,128)(2,1)} copy(bf16[1024,4096]{0,1:T(8,128)(2,1)} %fusion) | data formatting | bytes 16777216
  478.6 7.9 %all-gather.11.cloned.1.call-done = bf16[1024,4096]{1,0:T(8,128)(2,1)} async-done(((bf16[128,4096]{1,0:T(8,128)(2,1)}), bf16[1024,4096]{1,0:T(8,128)(2,1)}) %all-gather.11.cloned.1.call-update) | async-done | bytes 8388624 | tf_op jit(solution)/shard_map/all_gather | solution.py:58
  486.5 14.6 %multiply_convert_fusion = bf16[4096,1024]{1,0:T(8,128)(2,1)} fusion(bf16[1024,4096]{1,0:T(8,128)(2,1)} %all-gather.11.cloned.1.call-done, bf16[1024,1024]{1,0:T(8,128)(2,1)S(1)} %copy-done.3), kind=kOutput, calls=%fused_computation.1 | convolution fusion | flops 8598323200 | bytes 18874368 | tf_op jit(solution)/shard_map/dot_general | solution.py:62
  501.1 39.5 %reduce-scatter.5.cloned.1.call-done = f32[256,1024]{1,0:T(8,128)} async-done(((f32[1024,1024]{1,0:T(8,128)}), f32[256,1024]{1,0:T(8,128)}) %reduce-scatter.5.cloned.1.call-update) | async-done | bytes 1048592 | tf_op jit(solution)/shard_map/reduce_scatter | solution.py:78
  540.6 2.1 convert_element_type.37
  (31 shorter events, 1.0 us)
Async XLA Ops:
  7.2 40.7 %all-gather.5.cloned.1.call-start = ((), (), s32[]{:S(2)}) async-start(), calls=%async_computation.2 | async-start | bytes 2621440 | tf_op jit(solution)/shard_map/all_gather | solution.py:45
  7.9 224.5 %reduce-scatter.3.cloned.1.call-start = ((), (), s32[]{:S(2)}) async-start(), calls=%async_computation.3 | async-start | bytes 18874368 | tf_op jit(solution)/shard_map/reduce_scatter | solution.py:51
  63.9 168.4 %copy-start.1 = (bf16[128,4096]{1,0:T(8,128)(2,1)S(1)}, bf16[128,4096]{1,0:T(8,128)(2,1)}, u32[]{:S(2)}) copy-start(bf16[128,4096]{1,0:T(8,128)(2,1)} %param.9) | copy-start | bytes 3145732
  63.9 168.4 %copy-start.2 = (bf16[128,4096]{1,0:T(8,128)(2,1)S(1)}, bf16[128,4096]{1,0:T(8,128)(2,1)}, u32[]{:S(2)}) copy-start(bf16[128,4096]{1,0:T(8,128)(2,1)} %param.10) | copy-start | bytes 3145732
  64.0 334.7 %all-gather.7.cloned.1.call-start = ((), (), s32[]{:S(2)}) async-start(), calls=%async_computation.4 | async-start | bytes 9437184 | tf_op jit(solution)/shard_map/all_gather | solution.py:59
  236.5 188.0 %all-gather.9.cloned.1.call-start = ((), (), s32[]{:S(2)}) async-start(), calls=%async_computation.6 | async-start | bytes 2621440 | tf_op jit(solution)/shard_map/all_gather | solution.py:44
  237.1 249.4 %all-gather.11.cloned.1.call-start = ((), (), s32[]{:S(2)}) async-start(), calls=%async_computation.7 | async-start | bytes 9437184 | tf_op jit(solution)/shard_map/all_gather | solution.py:58
  237.2 26.8 %collective-permute-start = (bf16[128,4096]{1,0:T(8,128)(2,1)S(1)}, bf16[128,4096]{1,0:T(8,128)(2,1)S(1)}, u32[]{:S(2)}, u32[]{:S(2)}) collective-permute-start(bf16[128,4096]{1,0:T(8,128)(2,1)S(1)} %get-tuple-element.8), channel_id=1, source_target_pairs={{0,4},{4,8},{8,12},{12,16},{16,20},{20,24},{24,28},{28,0},{1,5},{5... | collective-permute-start | bytes 3145736 | tf_op jit(solution)/shard_map/ppermute | solution.py:20
  264.0 49.3 %collective-permute-start.1 = (bf16[128,4096]{1,0:T(8,128)(2,1)S(1)}, bf16[128,4096]{1,0:T(8,128)(2,1)S(1)}, u32[]{:S(2)}, u32[]{:S(2)}) collective-permute-start(bf16[128,4096]{1,0:T(8,128)(2,1)S(1)} %collective-permute-done), channel_id=1, source_target_pairs={{0,4},{4,8},{8,12},{12,16},{16,20},{20,24},{24,28},{28,0},{1,5},{5... | collective-permute-start | bytes 3145736 | tf_op jit(solution)/shard_map/ppermute | solution.py:20
  264.0 276.6 %reduce-scatter.5.cloned.1.call-start = ((), (), s32[]{:S(2)}) async-start(), calls=%async_computation.5 | async-start | bytes 5242880 | tf_op jit(solution)/shard_map/reduce_scatter | solution.py:78
  264.1 49.2 %collective-permute-start.4 = (bf16[128,4096]{1,0:T(8,128)(2,1)S(1)}, bf16[128,4096]{1,0:T(8,128)(2,1)}, u32[]{:S(2)}, u32[]{:S(2)}) collective-permute-start(bf16[128,4096]{1,0:T(8,128)(2,1)S(1)} %get-tuple-element.8), channel_id=1, source_target_pairs={{4,0},{8,4},{12,8},{16,12},{20,16},{24,20},{28,24},{0,28},{5,1},{9... | collective-permute-start | bytes 3145736 | tf_op jit(solution)/shard_map/ppermute | solution.py:22
  313.3 39.7 %collective-permute-start.2 = (bf16[128,4096]{1,0:T(8,128)(2,1)S(1)}, bf16[128,4096]{1,0:T(8,128)(2,1)}, u32[]{:S(2)}, u32[]{:S(2)}) collective-permute-start(bf16[128,4096]{1,0:T(8,128)(2,1)S(1)} %collective-permute-done.1), channel_id=1, source_target_pairs={{0,4},{4,8},{8,12},{12,16},{16,20},{20,24},{24,28},{28,0},{1,5},{5... | collective-permute-start | bytes 3145736 | tf_op jit(solution)/shard_map/ppermute | solution.py:20
  313.3 48.7 %collective-permute-start.5 = (bf16[128,4096]{1,0:T(8,128)(2,1)}, bf16[128,4096]{1,0:T(8,128)(2,1)}, u32[]{:S(2)}, u32[]{:S(2)}) collective-permute-start(bf16[128,4096]{1,0:T(8,128)(2,1)} %collective-permute-done.4), channel_id=1, source_target_pairs={{4,0},{8,4},{12,8},{16,12},{20,16},{24,20},{28,24},{0,28},{5,1},{9... | collective-permute-start | bytes 3145736 | tf_op jit(solution)/shard_map/ppermute | solution.py:22
  352.9 24.2 %collective-permute-start.3 = (bf16[128,4096]{1,0:T(8,128)(2,1)}, bf16[128,4096]{1,0:T(8,128)(2,1)}, u32[]{:S(2)}, u32[]{:S(2)}) collective-permute-start(bf16[128,4096]{1,0:T(8,128)(2,1)} %collective-permute-done.2), channel_id=1, source_target_pairs={{0,4},{4,8},{8,12},{12,16},{16,20},{20,24},{24,28},{28,0},{1,5},{5... | collective-permute-start | bytes 3145736 | tf_op jit(solution)/shard_map/ppermute | solution.py:20
  362.0 27.4 %collective-permute-start.6 = (bf16[128,4096]{1,0:T(8,128)(2,1)}, bf16[128,4096]{1,0:T(8,128)(2,1)S(1)}, u32[]{:S(2)}, u32[]{:S(2)}) collective-permute-start(bf16[128,4096]{1,0:T(8,128)(2,1)} %collective-permute-done.5), channel_id=1, source_target_pairs={{4,0},{8,4},{12,8},{16,12},{20,16},{24,20},{28,24},{0,28},{5,1},{9... | collective-permute-start | bytes 3145736 | tf_op jit(solution)/shard_map/ppermute | solution.py:22
  398.7 12.8 %copy-start = (bf16[8,128,4096]{2,1,0:T(8,128)(2,1)S(1)}, bf16[8,128,4096]{2,1,0:T(8,128)(2,1)}, u32[]{:S(2)}) copy-start(bf16[8,128,4096]{2,1,0:T(8,128)(2,1)} %gather_fusion) | copy-start | bytes 25165828
  439.8 12.1 %copy-start.4 = (bf16[1024,1024]{1,0:T(8,128)(2,1)S(1)}, bf16[1024,1024]{1,0:T(8,128)(2,1)}, u32[]{:S(2)}) copy-start(bf16[1024,1024]{1,0:T(8,128)(2,1)} %all-gather.9.cloned.1.call-done) | copy-start | bytes 6291460
  466.6 19.9 %copy-start.3 = (bf16[1024,1024]{1,0:T(8,128)(2,1)S(1)}, bf16[1024,1024]{1,0:T(8,128)(2,1)}, u32[]{:S(2)}) copy-start(bf16[1024,1024]{1,0:T(8,128)(2,1)} %all-gather.5.cloned.1.call-done) | copy-start | bytes 6291460
Sparse Core Ops, SparseCore 0:
  9.8 38.0 all-gather.4
  64.1 168.2 reduce-scatter.2
  236.7 127.3 all-gather.6
  365.8 37.1 all-gather.8
  404.4 82.0 all-gather.10
  489.3 51.2 reduce-scatter.4
